TPU v7x, 256 devices: a whole 4x4x8 slice. The times are simulated.
256 devices in a mesh: rep: 4 (over z_hi, core), ep: 64 (over z_lo, y, x).
Axes of the slice: x: 4, y: 4, z: 8 (z_hi: 2, z_lo: 4; z = z_hi * 4 + z_lo), core: 2. Of those that a mesh axis runs over, the one named last changes fastest.
Arguments:
- tokens: bfloat16 [4096, 3584], P('ep', 'rep'), may hold values from -6 to 6
- route_ids: int32 [4096, 8], P('ep'), may hold values from 0 to 127, all different within a row; in each aligned block of 64 rows (0 to 63, 64 to 127, ...) at most 6 rows name the same one
- route_weights: float32 [4096, 8], P('ep'), may hold values from 0.05 to 0.5
- swap_plan: int32 [64, 2], replicated, may hold values from 0 to 63, as said below
- gate_up: bfloat16 [128, 3584, 2, 1024], P('ep', None, None, 'rep'), may hold values from -0.09375 to 0.09375
- down: bfloat16 [128, 1024, 3584], P('ep', 'rep'), may hold values from -0.1875 to 0.1875
Outputs:
- mixed: bfloat16 [4096, 3584], P('ep', 'rep')
Inputs may be any that keep to these rules, and one draw needn't show every extreme that they name: swap_plan[d, 0] is d or the index 32 away from d (d + 64 / 2 modulo 64), and the pairing is mutual; swap_plan[d, 1] is a local slot below 2; at least one pair swaps. `route_ids`: each row names 8 different slots; among the rows of one index of ep no slot is named by more than 6 rows, a bound that some blocks reach.
All inputs are finite; a program needn't handle non-finite values.
Results may differ from a plain program's by a relative error of at most 0.012.
Values may be sent and summed in bfloat16 or wider, within the bound.
No kernel may reach another device: no remote copies, remote signals or barrier semaphores. Data moves between devices by JAX's collectives and lax.ppermute only.
A program may use at most 128 MiB of HBM per device.

v0:
```python
import jax
import jax.numpy as jnp
from jax import lax
from jax.sharding import PartitionSpec as P


def from_partner(value, axis, bit):
    return lax.ppermute(value, axis, [(i, i ^ 1 << bit) for i in range(lax.axis_size(axis))])


def shards(tokens, route_ids, route_weights, swap_plan, gate_up, down):
    ep_size = lax.axis_size("ep")
    my_index = lax.axis_index("ep")
    exp_dev = gate_up.shape[0]
    experts = exp_dev * ep_size
    tok_dev, top_k = route_ids.shape
    routed = tok_dev * top_k
    capacity = max(2, (routed * 3 + 2 * experts - 1) // (2 * experts))
    source = lax.all_gather(tokens, "rep", axis=1, tiled=True)
    row_width = source.shape[1]
    flat_ids = route_ids.reshape(routed)
    catalog = jnp.arange(experts, dtype=jnp.int32)
    my_partner = swap_plan[my_index, 0]
    my_slot = swap_plan[my_index, 1]
    moving = my_partner != my_index
    outgoing = (
        lax.dynamic_index_in_dim(gate_up, my_slot, 0, keepdims=False),
        lax.dynamic_index_in_dim(down, my_slot, 0, keepdims=False),
    )
    arrived = from_partner((outgoing[0], outgoing[1]), "ep", ep_size.bit_length() - 2)
    gate_list = [
        jnp.where(moving & (my_slot == index), arrived[0], gate_up[index])
        for index in range(exp_dev)
    ]
    down_list = [
        jnp.where(moving & (my_slot == index), arrived[1], down[index]) for index in range(exp_dev)
    ]
    one_hot = (flat_ids[:, None] == catalog[None, :]).astype(jnp.int32)
    position = jnp.sum(jnp.cumsum(one_hot, axis=0) * one_hot, axis=1) - 1
    slot_index = flat_ids * capacity + position
    outgoing_rows = (
        jnp.zeros((experts * capacity, row_width), jnp.bfloat16)
        .at[slot_index]
        .set(jnp.repeat(source, top_k, axis=0))
    )
    outgoing_rows = outgoing_rows.reshape(ep_size, exp_dev, capacity, row_width)
    full_rows = lax.all_to_all(outgoing_rows, "ep", split_axis=0, concat_axis=0, tiled=True)
    results = []
    for index in range(exp_dev):
        projected = jnp.einsum(
            "scd,dgf->scgf",
            full_rows[:, index],
            gate_list[index],
            preferred_element_type=jnp.float32,
        )
        hidden = (jax.nn.silu(projected[:, :, 0]) * projected[:, :, 1]).astype(jnp.bfloat16)
        results.append(
            jnp.einsum(
                "scf,fd->scd", hidden, down_list[index], preferred_element_type=jnp.float32
            ).astype(jnp.bfloat16)
        )
    returned = lax.all_to_all(
        jnp.stack(results, axis=1), "ep", split_axis=0, concat_axis=0, tiled=True
    )
    picked = returned.reshape(experts * capacity, returned.shape[3])[slot_index]
    summed_rows = lax.psum_scatter(
        picked.astype(jnp.float32).astype(jnp.bfloat16), "rep", scatter_dimension=1, tiled=True
    )
    weighted = (
        summed_rows.reshape(tok_dev, top_k, summed_rows.shape[1]).astype(jnp.float32)
        * route_weights[:, :, None]
    )
    return jnp.sum(weighted, axis=1).astype(jnp.bfloat16)


def solution(mesh):
    return jax.shard_map(
        shards,
        mesh=mesh,
        in_specs=(
            P("ep", "rep"),
            P("ep", None),
            P("ep", None),
            P(),
            P("ep", None, None, "rep"),
            P("ep", "rep", None),
        ),
        out_specs=P("ep", "rep"),
        check_vma=False,
    )
```

profile of v0, /device:TPU:2, one launch (start us, length us, event | category | flops | bytes accessed | tf_op | source)
XLA Modules:
  0.0 688.0 jit_solution(17708159407236667270)
XLA Ops:
  6.5 0.8 copy.41
  7.3 0.1 eq.37
  7.4 0.1 eq.33
  7.5 0.7 broadcast_multiply_fusion
  8.2 0.1 copy.43
  8.3 0.2 fusion.24
  8.6 0.2 fusion.23
  8.9 0.1 copy.40
  8.9 0.1 mul.42
  9.0 12.8 %all_gather.3 = bf16[64,3584]{1,0:T(8,128)(2,1)S(1)} all-gather(bf16[64,896]{1,0:T(8,128)(2,1)} %param.6), channel_id=1, replica_groups=mesh['rep'=4,'ep'=64] {'rep'}, dimensions={1}, use_global_device_ids=true | all-gather | bytes 573440 | tf_op jit(solution)/shard_map/all_gather | solution.py:19
  21.9 8.7 %scatter_custom_fusion = bf16[768,3584]{1,0:T(8,128)(2,1)} fusion(s32[512]{0:T(512)S(1)} %bitcast.97, bf16[]{:T(256)} %constant.11.clone.1, bf16[64,3584]{1,0:T(8,128)(2,1)S(1)} %all_gather.3), kind=kCustom, calls=%fused_computation.14 | custom fusion | bytes 5963778 | tf_op jit(solution)/shard_map/scatter | solution.py:44
  30.5 9.6 %reshape.66 = bf16[64,2,6,3584]{3,2,1,0:T(8,128)(2,1)} reshape(bf16[768,3584]{1,0:T(8,128)(2,1)} %scatter_custom_fusion) | data formatting | bytes 11010048 | tf_op jit(solution)/shard_map/reshape | solution.py:46
  40.1 9.4 %copy.45 = bf16[64,2,6,3584]{3,1,2,0:T(2,128)(2,1)} copy(bf16[64,2,6,3584]{3,2,1,0:T(8,128)(2,1)} %reshape.66) | data formatting | bytes 11010048 | tf_op jit(solution)/shard_map/reshape | solution.py:46
  49.5 11.6 %all-to-all-start = ((bf16[64,2,6,3584]{3,1,2,0:T(2,128)(2,1)}), bf16[64,2,6,3584]{3,1,2,0:T(2,128)(2,1)}, u32[]{:S(2)}, u32[]{:S(2)}) async-start(bf16[64,2,6,3584]{3,1,2,0:T(2,128)(2,1)} %copy.45), calls=%async_computation | async-start | bytes 11010048 | tf_op jit(solution)/shard_map/all_to_all | solution.py:47
  61.2 0.0 copy-done.5
  61.2 0.7 constant_dynamic-slice_fusion
  63.8 0.0 copy-start.2
  63.8 7.2 %dynamic-slice_bitcast_fusion = bf16[3584,2,256]{2,1,0:T(2,128)(2,1)} fusion(bf16[2,3584,2,256]{3,2,1,0:T(2,128)(2,1)} %param.10, s32[]{:T(128)S(6)} %select_n.52), kind=kLoop, calls=%fused_computation.17 | loop fusion | bytes 7340036 | tf_op jit(solution)/shard_map/jit(dynamic_index_in_dim)/squeeze | solution.py:27
  71.0 2.5 collective-permute-start
  73.5 0.1 dynamic-slice_bitcast_fusion.1
  73.6 0.7 collective-permute-start.1
  76.2 303.3 %collective-permute-done = bf16[3584,2,256]{2,1,0:T(2,128)(2,1)} collective-permute-done((bf16[3584,2,256]{2,1,0:T(2,128)(2,1)}, bf16[3584,2,256]{2,1,0:T(2,128)(2,1)}, u32[]{:S(2)}, u32[]{:S(2)}) %collective-permute-start) | collective-permute-done | bytes 3670048 | tf_op jit(solution)/shard_map/ppermute | solution.py:8
  379.5 8.9 %broadcast_select_fusion.1 = (bf16[3584,2,256]{2,1,0:T(2,128)(2,1)}, bf16[3584,2,256,1]{2,1,0,3:T(2,128)(2,1)}) fusion(bf16[3584,2,256]{2,1,0:T(2,128)(2,1)} %collective-permute-done, pred[]{:T(512)S(6)} %and.9, bf16[2,3584,2,256]{3,2,1,0:T(2,128)(2,1)} %param.10, pred[]{:T(512)S(6)} %and.10), kind=kLoop, calls=%fused_computation.3 | loop fusion | flops 3670016 | bytes 18350082 | tf_op jit(solution)/shard_map/jit(_where)/select_n | solution.py:32
  388.5 0.0 all-to-all-done
  388.5 0.0 copy-start.1
  388.5 11.1 %fusion.33 = (bf16[64,1,6,3584]{3,1,2,0:T(2,128)(2,1)S(1)}, bf16[64,1,6,3584]{3,1,2,0:T(2,128)(2,1)S(1)}) fusion(bf16[64,2,6,3584]{3,1,2,0:T(2,128)(2,1)} %all-to-all-done), kind=kLoop, calls=%fused_computation.60 | loop fusion | bytes 11010048 | tf_op jit(solution)/shard_map/slice | solution.py:52
  399.6 1.6 fusion.5
  401.2 0.4 copy-done
  401.6 1.6 fusion.3
  403.2 14.7 %collective-permute-done.1 = bf16[256,3584]{1,0:T(8,128)(2,1)} collective-permute-done((bf16[256,3584]{1,0:T(8,128)(2,1)S(1)}, bf16[256,3584]{1,0:T(8,128)(2,1)}, u32[]{:S(2)}, u32[]{:S(2)}) %collective-permute-start.1) | collective-permute-done | bytes 1835040 | tf_op jit(solution)/shard_map/ppermute | solution.py:8
  418.0 0.0 copy-done.3
  418.0 0.9 fusion
  418.9 0.9 fusion.1
  419.8 0.5 pad_maximum_fusion
  420.3 11.4 %copy.53 = bf16[64,2,6,3584]{3,1,2,0:T(2,128)(2,1)} copy(bf16[64,2,6,3584]{3,0,2,1:T(8,128)(2,1)S(1)} %pad_maximum_fusion) | data formatting | bytes 11010048 | tf_op jit(solution)/shard_map/stack | solution.py:63
  431.7 13.5 %all-to-all-start.1 = ((bf16[64,2,6,3584]{3,1,2,0:T(2,128)(2,1)}), bf16[64,2,6,3584]{3,1,2,0:T(2,128)(2,1)}, u32[]{:S(2)}, u32[]{:S(2)}) async-start(bf16[64,2,6,3584]{3,1,2,0:T(2,128)(2,1)} %copy.53), calls=%async_computation.1 | async-start | bytes 11010048 | tf_op jit(solution)/shard_map/all_to_all | solution.py:62
  445.2 0.3 reduce-scatter.4.cloned.1.call-start
  445.5 122.7 %all-to-all-done.1 = bf16[64,2,6,3584]{3,1,2,0:T(2,128)(2,1)} async-done(((bf16[64,2,6,3584]{3,1,2,0:T(2,128)(2,1)}), bf16[64,2,6,3584]{3,1,2,0:T(2,128)(2,1)}, u32[]{:S(2)}, u32[]{:S(2)}) %all-to-all-start.1) | async-done | bytes 5505056 | tf_op jit(solution)/shard_map/all_to_all | solution.py:62
  568.2 7.3 %copy.54 = bf16[64,2,6,3584]{3,2,1,0:T(8,128)(2,1)} copy(bf16[64,2,6,3584]{3,1,2,0:T(2,128)(2,1)} %all-to-all-done.1) | data formatting | bytes 11010048 | tf_op jit(solution)/shard_map/all_to_all | solution.py:62
  575.5 9.7 %reshape.67 = bf16[768,3584]{1,0:T(8,128)(2,1)} reshape(bf16[64,2,6,3584]{3,2,1,0:T(8,128)(2,1)} %copy.54) | data formatting | bytes 11010048 | tf_op jit(solution)/shard_map/reshape | solution.py:65
  585.1 11.1 %gather_fusion = bf16[512,3584]{1,0:T(8,128)(2,1)} fusion(bf16[768,3584]{1,0:T(8,128)(2,1)} %reshape.67, s32[1024]{0:T(1024)S(1)} %pad_clamp_fusion), kind=kCustom, calls=%fused_computation | custom fusion | bytes 7342080 | tf_op jit(solution)/shard_map/gather | solution.py:65
  596.3 5.9 copy.61
  602.2 0.0 reduce-scatter.4.cloned.1.call-update
  602.2 0.7 copy-done.4
  602.9 0.1 copy.55
  603.0 75.4 %reduce-scatter.4.cloned.1.call-done = bf16[896,512]{1,0:T(8,128)(2,1)} async-done(((bf16[3584,512]{1,0:T(8,128)(2,1)}), bf16[896,512]{1,0:T(8,128)(2,1)}) %reduce-scatter.4.cloned.1.call-update) | async-done | bytes 917520
  678.3 1.5 copy.62
  679.9 1.3 fusion.11
  (15 shorter events, 0.1 us)
Async XLA Ops:
  49.5 11.7 %copy-start.5 = (s32[64,2]{0,1:T(2,128)S(1)}, s32[64,2]{0,1:T(2,128)}, u32[]{:S(2)}) copy-start(s32[64,2]{0,1:T(2,128)} %param.9) | copy-start | bytes 1540
  49.5 338.9 %all-to-all-start = ((bf16[64,2,6,3584]{3,1,2,0:T(2,128)(2,1)}), bf16[64,2,6,3584]{3,1,2,0:T(2,128)(2,1)}, u32[]{:S(2)}, u32[]{:S(2)}) async-start(bf16[64,2,6,3584]{3,1,2,0:T(2,128)(2,1)} %copy.45), calls=%async_computation | async-start | bytes 11010048 | tf_op jit(solution)/shard_map/all_to_all | solution.py:47
  63.8 9.7 %copy-start.2 = (bf16[2,256,3584]{2,1,0:T(8,128)(2,1)S(1)}, bf16[2,256,3584]{2,1,0:T(8,128)(2,1)}, u32[]{:S(2)}) copy-start(bf16[2,256,3584]{2,1,0:T(8,128)(2,1)} %param.11) | copy-start | bytes 11010052
  71.0 308.5 %collective-permute-start = (bf16[3584,2,256]{2,1,0:T(2,128)(2,1)}, bf16[3584,2,256]{2,1,0:T(2,128)(2,1)}, u32[]{:S(2)}, u32[]{:S(2)}) collective-permute-start(bf16[3584,2,256]{2,1,0:T(2,128)(2,1)} %dynamic-slice_bitcast_fusion), channel_id=1, source_target_pairs={{0,32},{1,33},{2,34},{3,35},{4,36},{5,37},{6,38},{7,39},{8,40},{9,... | collective-permute-start | bytes 11010056 | tf_op jit(solution)/shard_map/ppermute | solution.py:8
  73.6 344.4 %collective-permute-start.1 = (bf16[256,3584]{1,0:T(8,128)(2,1)S(1)}, bf16[256,3584]{1,0:T(8,128)(2,1)}, u32[]{:S(2)}, u32[]{:S(2)}) collective-permute-start(bf16[256,3584]{1,0:T(8,128)(2,1)S(1)} %dynamic-slice_bitcast_fusion.1), channel_id=1, source_target_pairs={{0,32},{1,33},{2,34},{3,35},{4,36},{5,37},{6,38},{7,39},{8,40},{9,... | collective-permute-start | bytes 5505032 | tf_op jit(solution)/shard_map/ppermute | solution.py:8
  388.5 11.1 %copy-start.1 = (bf16[3584,2,256]{2,1,0:T(2,128)(2,1)S(1)}, bf16[3584,2,256]{2,1,0:T(2,128)(2,1)}, u32[]{:S(2)}) copy-start(bf16[3584,2,256]{2,1,0:T(2,128)(2,1)} %get-tuple-element.5) | copy-start | bytes 11010052
  399.6 2.0 copy-start
  401.6 16.4 %copy-start.3 = (bf16[2,256,3584]{2,1,0:T(8,128)(2,1)S(1)}, bf16[2,256,3584]{2,1,0:T(8,128)(2,1)}, u32[]{:S(2)}) copy-start(bf16[2,256,3584]{2,1,0:T(8,128)(2,1)} %param.11) | copy-start | bytes 11010052
  431.7 136.5 %all-to-all-start.1 = ((bf16[64,2,6,3584]{3,1,2,0:T(2,128)(2,1)}), bf16[64,2,6,3584]{3,1,2,0:T(2,128)(2,1)}, u32[]{:S(2)}, u32[]{:S(2)}) async-start(bf16[64,2,6,3584]{3,1,2,0:T(2,128)(2,1)} %copy.53), calls=%async_computation.1 | async-start | bytes 11010048 | tf_op jit(solution)/shard_map/all_to_all | solution.py:62
  445.2 233.1 %reduce-scatter.4.cloned.1.call-start = ((), (), s32[]{:S(2)}) async-start(), calls=%async_computation.3 | async-start | bytes 4587520
  602.2 0.7 copy-start.4
Sparse Core Ops, SparseCore 0:
  602.3 75.9 reduce-scatter.3
where the time goes:
time: 690 us; the launch traced here: 688 us
  waiting for transfers between devices  516 us (75%)
  local copies, waits for them, and re-layouts  96.2 us (14%)
  starting transfers between devices  28.6 us (4%)
  between operations  17.4 us (3%)
  blocking collectives  12.8 us (2%)
  other arithmetic  11.9 us (2%)
    ppermute x2, waiting for transfers between devices, from_partner(): lax.ppermute(value, axis, [(i, i ^ 1 << bit) for i in range(lax.axis_size...  318 us
    all_to_all x1, waiting for transfers between devices, shards(): lax.all_to_all(jnp.stack(results, axis=1), 'ep', split_axis=0, concat_axi...  123 us
    unnamed x2, waiting for transfers between devices  75.4 us
    reshape x2, local copies, waits for them, and re-layouts, shards(): outgoing_rows = outgoing_rows.reshape(ep_size, exp_dev, capacity, row_width)  19 us
  transfers between devices with their start and end apart: 5, of which 4 were waited for; matrix products, arithmetic and copies ran while one was open for 5% of the time, Pallas kernels for 0%

commit v1 on v0

v1 whole, which is shorter than its diff:
```python
import jax
import jax.numpy as jnp
from jax import lax
from jax.sharding import PartitionSpec as P


def pair_swap(value, axis, bit):
    return lax.ppermute(value, axis, [(i, i ^ 1 << bit) for i in range(lax.axis_size(axis))])


def pick(flag, first, second):
    return jnp.where(flag, first, second), jnp.where(flag, second, first)


def holder_of(swap_plan, exp_dev):
    ep_size = swap_plan.shape[0]
    slot = jnp.arange(ep_size * exp_dev, dtype=jnp.int32)
    index = slot // exp_dev
    partner = swap_plan[index, 0]
    given = swap_plan[index, 1]
    moved = (partner != index) & (slot % exp_dev == given)
    return jnp.where(moved, partner * exp_dev + swap_plan[partner, 1], slot)


def shards(tokens, route_ids, route_weights, swap_plan, gate_up, down):
    ep_size = lax.axis_size("ep")
    rep = lax.axis_index("rep")
    core = rep % 2
    half = rep // 2
    exp_dev = gate_up.shape[0]
    experts = exp_dev * ep_size
    tok_dev, top_k = route_ids.shape
    routed = tok_dev * top_k
    capacity = max(2, (routed * 3 + 2 * experts - 1) // (2 * experts))
    places = experts * capacity
    width = tokens.shape[1]

    holder = holder_of(swap_plan, exp_dev)
    owners = holder[route_ids.reshape(routed)]
    catalog = jnp.arange(experts, dtype=jnp.int32)
    one_hot = (owners[:, None] == catalog[None, :]).astype(jnp.float32)
    earlier = (jnp.arange(routed)[:, None] > jnp.arange(routed)[None, :]).astype(jnp.float32)
    before = jnp.dot(earlier, one_hot, preferred_element_type=jnp.float32)
    position = jnp.sum(before * one_hot, axis=1).astype(jnp.int32)
    place = owners * capacity + position
    hits = (place[:, None] == jnp.arange(places, dtype=jnp.int32)[None, :]).reshape(tok_dev, top_k, places)
    gather = jnp.sum(hits.astype(jnp.bfloat16), axis=1)
    mixing = jnp.sum(jnp.where(hits, route_weights[:, :, None], 0.0), axis=1)

    other = pair_swap(tokens, "rep", 1)
    low, high = pick(half == 0, tokens, other)
    features = jnp.stack([low, high], axis=1).reshape(tok_dev, 2 * width)
    outgoing = lax.dot_general(
        gather, features, (((0,), (0,)), ((), ())), preferred_element_type=jnp.float32
    ).astype(jnp.bfloat16)
    outgoing = outgoing.reshape(ep_size, exp_dev * capacity, 2 * width)
    arrived = lax.all_to_all(outgoing, "ep", split_axis=0, concat_axis=0, tiled=True)

    mine = arrived.reshape(ep_size, exp_dev * capacity, 2, width)
    theirs = pair_swap(mine, "rep", 0)
    first, second = pick(core == 0, mine, theirs)
    rows = jnp.stack([first, second], axis=3).reshape(ep_size, exp_dev, capacity, 4 * width)

    results = []
    for index in range(exp_dev):
        projected = jnp.einsum(
            "scd,dgf->scgf", rows[:, index], gate_up[index], preferred_element_type=jnp.float32
        )
        hidden = (jax.nn.silu(projected[:, :, 0]) * projected[:, :, 1]).astype(jnp.bfloat16)
        results.append(
            jnp.einsum(
                "scf,fd->scd", hidden, down[index], preferred_element_type=jnp.float32
            ).astype(jnp.bfloat16)
        )
    partial = jnp.stack(results, axis=1).reshape(ep_size, exp_dev * capacity, 2, 2, width)

    keep, send = pick(core == 0, partial[:, :, :, 0], partial[:, :, :, 1])
    paired = (keep.astype(jnp.float32) + pair_swap(send, "rep", 0).astype(jnp.float32)).astype(
        jnp.bfloat16
    )
    returned = lax.all_to_all(
        paired.reshape(ep_size, exp_dev * capacity, 2 * width), "ep", split_axis=0, concat_axis=0, tiled=True
    )
    weighted = jnp.dot(
        mixing,
        returned.reshape(places, 2 * width).astype(jnp.float32),
        precision=lax.Precision.HIGHEST,
        preferred_element_type=jnp.float32,
    ).reshape(tok_dev, 2, width)
    own, away = pick(half == 0, weighted[:, 0], weighted[:, 1])
    return (own + pair_swap(away, "rep", 1)).astype(jnp.bfloat16)


def solution(mesh):
    return jax.shard_map(
        shards,
        mesh=mesh,
        in_specs=(
            P("ep", "rep"),
            P("ep", None),
            P("ep", None),
            P(),
            P("ep", None, None, "rep"),
            P("ep", "rep", None),
        ),
        out_specs=P("ep", "rep"),
        check_vma=False,
    )
```

time: 690 us -> 334 us (0.48)
  waiting for transfers between devices: 516 us -> 101 us
  blocking collectives: 12.8 us -> 93.2 us
  between operations: 17.4 us -> 0.31 us
  starting transfers between devices: 28.6 us -> 15.8 us
  other arithmetic: 11.9 us -> 21.9 us
  local copies, waits for them, and re-layouts: 96.2 us -> 88.6 us
    ppermute x2 -> x4, waiting for transfers between devices: 318 us -> 17.3 us  [pair_swap(): lax.ppermute(value, axis, [(i, i ^ 1 << bit) for i in range(lax.axis_size...]
    all_to_all x0 -> x1, blocking collectives: none -> 93.2 us  [shards(): lax.all_to_all(outgoing, 'ep', split_axis=0, concat_axis=0, tiled=True)]
    unnamed x2 -> x0, waiting for transfers between devices: 75.4 us -> none
    all_to_all x2 -> x1, waiting for transfers between devices: 123 us -> 83.8 us  [shards(): lax.all_to_all(paired.reshape(ep_size, exp_dev * capacity, 2 * width), 'e...]
    reshape x3 -> x10, local copies, waits for them, and re-layouts: 28.7 us -> 48.2 us  [the longest x1 12.6 us: shards(): jnp.stack([first, second], axis=3)]
    all_to_all x2 -> x1, starting transfers between devices: 25.2 us -> 6.31 us  [shards(): lax.all_to_all(paired.reshape(ep_size, exp_dev * capacity, 2 * width), 'e...]
    another operation x4, other arithmetic: 0.76 us -> 17.8 us  [the longest x2 14.8 us: shards(): jnp.stack([first, second], axis=3)]
    all_gather x1 -> x0, blocking collectives: 12.8 us -> none  [shards(): source = lax.all_gather(tokens, 'rep', axis=1, tiled=True)]
  transfers between devices with their start and end apart: 5 -> 5, of which waited for: 4 -> 3; matrix products, arithmetic and copies ran while one was open for 5% -> 5% of each run, Pallas kernels for 0% -> 0%
where the time goes in v1:
time: 334 us; the launch traced here: 333 us
  waiting for transfers between devices  101 us (30%)
  blocking collectives  93.2 us (28%)
  local copies, waits for them, and re-layouts  88.6 us (27%)
  other arithmetic  21.9 us (7%)
  starting transfers between devices  15.8 us (5%)
  matrix products  11.8 us (4%)
    all_to_all x1, blocking collectives, shards(): lax.all_to_all(outgoing, 'ep', split_axis=0, concat_axis=0, tiled=True)  93.2 us
    all_to_all x1, waiting for transfers between devices, shards(): lax.all_to_all(paired.reshape(ep_size, exp_dev * capacity, 2 * width), 'e...  83.8 us
    ppermute x4, waiting for transfers between devices, pair_swap(): lax.ppermute(value, axis, [(i, i ^ 1 << bit) for i in range(lax.axis_size...  17.3 us
    another operation x2, other arithmetic, shards(): jnp.stack([first, second], axis=3)  14.8 us
    slice x1, local copies, waits for them, and re-layouts, shards(): keep, send = pick(core == 0, partial[:, :, :, 0], partial[:, :, :, 1])  13.6 us
    reshape x1, local copies, waits for them, and re-layouts, shards(): jnp.stack([first, second], axis=3)  12.6 us
    reshape x1, local copies, waits for them, and re-layouts, shards(): jnp.stack(results, axis=1).reshape(ep_size, exp_dev * capacity, 2, 2, width)  11.8 us
    reshape x2, local copies, waits for them, and re-layouts, shards(): mine = arrived.reshape(ep_size, exp_dev * capacity, 2, width)  9.73 us
  transfers between devices with their start and end apart: 5, of which 3 were waited for; matrix products, arithmetic and copies ran while one was open for 5% of the time, Pallas kernels for 0%

profile of v1, /device:TPU:2, one launch (start us, length us, event | category | flops | bytes accessed | tf_op | source)
XLA Modules:
  0.0 332.7 jit_solution(17674014384325731053)
XLA Ops:
  0.0 7.2 %collective-permute-start = (bf16[64,896]{1,0:T(8,128)(2,1)}, bf16[64,896]{1,0:T(8,128)(2,1)S(1)}, u32[]{:S(2)}, u32[]{:S(2)}) collective-permute-start(bf16[64,896]{1,0:T(8,128)(2,1)} %param.6), channel_id=1, source_target_pairs={{0,128},{64,192},{128,0},{192,64},{1,129},{65,193},{129,1},{193,65... | collective-permute-start | bytes 344072 | tf_op jit(solution)/shard_map/ppermute | solution.py:8
  7.3 1.5 gather_fusion
  8.8 1.5 gather_fusion.2
  10.3 1.5 gather_fusion.1
  11.8 0.8 copy.59
  12.6 0.1 reshape.146
  12.7 3.3 %gather_fusion.3 = s32[512]{0:T(512)S(1)} fusion(s32[128]{0:T(128)S(1)} %and_select_fusion, s32[1024]{0:T(1024)S(1)} %pad_clamp_fusion), kind=kCustom, calls=%fused_computation.3 | custom fusion | bytes 6144 | tf_op jit(solution)/shard_map/gather | solution.py:39
  16.1 0.3 fusion.12
  16.4 0.1 add.96
  16.5 0.5 fusion.13
  17.0 0.0 collective-permute-done
  17.1 0.9 convolution_convert_fusion.2
  18.0 2.5 reshape.148
  20.5 93.2 %all_to_all.10 = bf16[64,12,1792]{2,1,0:T(8,128)(2,1)} all-to-all(bf16[64,12,1792]{2,1,0:T(8,128)(2,1)} %reshape.148), channel_id=1, replica_groups=mesh['rep'=4,'ep'=64] {'ep'}, dimensions={0} | all-to-all | bytes 5505024 | tf_op jit(solution)/shard_map/all_to_all | solution.py:57
  113.8 5.7 %reshape.188 = bf16[64,12,2,896]{3,2,1,0:T(2,128)(2,1)S(1)} reshape(bf16[64,12,1792]{2,1,0:T(8,128)(2,1)} %all_to_all.10) | data formatting | bytes 5505024 | tf_op jit(solution)/shard_map/reshape | solution.py:59
  119.5 4.0 %copy.75 = bf16[64,12,2,896]{3,2,0,1:T(2,128)(2,1)} copy(bf16[64,12,2,896]{3,2,1,0:T(2,128)(2,1)S(1)} %reshape.188) | data formatting | bytes 5505024 | tf_op jit(solution)/shard_map/reshape | solution.py:59
  123.5 0.0 collective-permute-start.1
  123.5 7.6 %fusion.33 = (bf16[1,3584,2,256]{3,2,1,0:T(2,128)(2,1)}, bf16[1,3584,2,256]{3,2,1,0:T(2,128)(2,1)}) fusion(bf16[2,3584,2,256]{3,2,1,0:T(2,128)(2,1)} %param.10), kind=kLoop, calls=%fused_computation.76 | loop fusion | bytes 14680064 | tf_op jit(solution)/shard_map/slice | solution.py:67
  131.1 0.0 collective-permute-done.1
  131.1 6.0 %fusion.5 = (bf16[64,12,2,1,896]{4,2,0,1,3:T(2,128)(2,1)S(1)}, bf16[64,12,2,1,896]{4,2,0,1,3:T(2,128)(2,1)S(1)}) fusion(bf16[64,12,2,896]{3,2,0,1:T(2,128)(2,1)} %collective-permute-done.1, pred[]{:T(512)S(6)} %eq.50, bf16[64,12,2,896]{3,2,1,0:T(2,128)(2,1)S(1)} %reshape.188), kind=kLoop, calls=%fused_computation.19 | loop fusion | flops 2752512 | bytes 11010049 | tf_op jit(solution)/shard_map/stack | solution.py:62
  137.1 8.9 %pad_maximum_fusion = bf16[64,12,2,2,896]{4,2,0,1,3:T(2,128)(2,1)S(1)} fusion(bf16[64,12,2,1,896]{4,2,0,1,3:T(2,128)(2,1)S(1)} %get-tuple-element.10, bf16[64,12,2,1,896]{4,2,0,1,3:T(2,128)(2,1)S(1)} %get-tuple-element.9), kind=kLoop, calls=%fused_computation.6 | loop fusion | flops 2752512 | bytes 11010048 | tf_op jit(solution)/shard_map/stack | solution.py:62
  146.0 5.6 %copy.65 = bf16[64,12,2,2,896]{4,3,2,0,1:T(2,128)(2,1)} copy(bf16[64,12,2,2,896]{4,2,0,1,3:T(2,128)(2,1)S(1)} %pad_maximum_fusion) | data formatting | bytes 11010048 | tf_op jit(solution)/shard_map/stack | solution.py:62
  151.6 12.6 %reshape.150 = bf16[64,2,6,3584]{3,0,2,1:T(8,128)(2,1)} reshape(bf16[64,12,2,2,896]{4,3,2,0,1:T(2,128)(2,1)} %copy.65) | data formatting | bytes 11010048 | tf_op jit(solution)/shard_map/reshape | solution.py:62
  164.2 4.6 %fusion.4 = f32[64,6,2,256]{3,0,2,1:T(8,128)S(1)} fusion(bf16[1,3584,2,256]{3,2,1,0:T(2,128)(2,1)} %get-tuple-element.5, bf16[64,2,6,3584]{3,0,2,1:T(8,128)(2,1)} %reshape.150), kind=kOutput, calls=%fused_computation.17 | convolution fusion | flops 1409286144 | bytes 7208960 | tf_op jit(solution)/shard_map/scd,dgf->scgf/dot_general | solution.py:66
  168.8 0.9 copy-done.3
  169.7 1.6 fusion.3
  171.3 0.5 copy-done.6
  171.8 0.9 fusion.1
  172.7 0.9 fusion.2
  173.6 2.9 pad_maximum_fusion.1
  176.5 11.8 %reshape.151 = bf16[64,12,2,2,896]{4,3,2,0,1:T(2,128)(2,1)} reshape(bf16[64,2,6,3584]{3,0,2,1:T(8,128)(2,1)} %pad_maximum_fusion.1) | data formatting | bytes 11010048 | tf_op jit(solution)/shard_map/reshape | solution.py:75
  188.3 13.6 %fusion.34 = (bf16[64,12,2,1,896]{4,3,2,0,1:T(2,128)(2,1)S(1)}, bf16[64,12,2,1,896]{4,3,2,0,1:T(2,128)(2,1)S(1)}) fusion(bf16[64,12,2,2,896]{4,3,2,0,1:T(2,128)(2,1)} %reshape.151), kind=kLoop, calls=%fused_computation.77 | loop fusion | bytes 11010048 | tf_op jit(solution)/shard_map/slice | solution.py:77
  201.9 0.8 select_bitcast_fusion
  202.7 0.8 collective-permute-start.2
  203.5 4.7 %collective-permute-done.2 = bf16[64,12,2,896]{3,0,2,1:T(8,128)(2,1)S(1)} collective-permute-done((bf16[64,12,2,896]{3,0,2,1:T(8,128)(2,1)S(1)}, bf16[64,12,2,896]{3,0,2,1:T(8,128)(2,1)S(1)}, u32[]{:S(2)}, u32[]{:S(2)}) %collective-permute-start.2) | collective-permute-done | bytes 2752544 | tf_op jit(solution)/shard_map/ppermute | solution.py:8
  208.2 1.5 fusion
  209.7 2.8 copy.77
  212.6 3.3 reshape.189
  215.9 6.3 %all-to-all-start.1 = ((bf16[64,12,1792]{2,1,0:T(8,128)(2,1)}), bf16[64,12,1792]{2,1,0:T(8,128)(2,1)}, u32[]{:S(2)}, u32[]{:S(2)}) async-start(bf16[64,12,1792]{2,1,0:T(8,128)(2,1)} %reshape.189), calls=%async_computation.1 | async-start | bytes 7340032 | tf_op jit(solution)/shard_map/all_to_all | solution.py:81
  222.2 0.1 copy.60
  222.3 0.5 select_reduce_fusion
  222.9 83.8 %all-to-all-done.1 = bf16[64,12,1792]{2,1,0:T(8,128)(2,1)} async-done(((bf16[64,12,1792]{2,1,0:T(8,128)(2,1)}), bf16[64,12,1792]{2,1,0:T(8,128)(2,1)}, u32[]{:S(2)}, u32[]{:S(2)}) %all-to-all-start.1) | async-done | bytes 2752544 | tf_op jit(solution)/shard_map/all_to_all | solution.py:81
  306.6 5.4 %reshape.153 = bf16[768,1792]{1,0:T(8,128)(2,1)} reshape(bf16[64,12,1792]{2,1,0:T(8,128)(2,1)} %all-to-all-done.1) | data formatting | bytes 5505024 | tf_op jit(solution)/shard_map/reshape | solution.py:86
  312.0 3.3 %copy.72 = bf16[1792,768]{1,0:T(8,128)(2,1)S(1)} copy(bf16[1792,768]{0,1:T(8,128)(2,1)} %bitcast.84) | data formatting | bytes 5505024 | tf_op jit(solution)/shard_map/dot_general | solution.py:84
  315.3 2.6 fusion.19
  318.0 1.5 collective-permute-start.3
  319.5 12.5 %collective-permute-done.3 = f32[64,896]{1,0:T(8,128)S(1)} collective-permute-done((f32[64,896]{1,0:T(8,128)S(1)}, f32[64,896]{1,0:T(8,128)S(1)}, u32[]{:S(2)}, u32[]{:S(2)}) %collective-permute-start.3) | collective-permute-done | bytes 229408 | tf_op jit(solution)/shard_map/ppermute | solution.py:8
  332.0 0.7 fusion.16
  (23 shorter events, 0.2 us)
Async XLA Ops:
  0.0 7.2 %copy-start = (s32[64,2]{0,1:T(2,128)S(1)}, s32[64,2]{0,1:T(2,128)}, u32[]{:S(2)}) copy-start(s32[64,2]{0,1:T(2,128)} %param.9) | copy-start | bytes 1540
  0.0 17.0 %copy-start.4 = (bf16[64,896]{1,0:T(8,128)(2,1)S(1)}, bf16[64,896]{1,0:T(8,128)(2,1)}, u32[]{:S(2)}) copy-start(bf16[64,896]{1,0:T(8,128)(2,1)} %param.6) | copy-start | bytes 344068
  0.0 17.0 %collective-permute-start = (bf16[64,896]{1,0:T(8,128)(2,1)}, bf16[64,896]{1,0:T(8,128)(2,1)S(1)}, u32[]{:S(2)}, u32[]{:S(2)}) collective-permute-start(bf16[64,896]{1,0:T(8,128)(2,1)} %param.6), channel_id=1, source_target_pairs={{0,128},{64,192},{128,0},{192,64},{1,129},{65,193},{129,1},{193,65... | collective-permute-start | bytes 344072 | tf_op jit(solution)/shard_map/ppermute | solution.py:8
  123.5 7.6 %collective-permute-start.1 = (bf16[64,12,2,896]{3,2,0,1:T(2,128)(2,1)}, bf16[64,12,2,896]{3,2,0,1:T(2,128)(2,1)}, u32[]{:S(2)}, u32[]{:S(2)}) collective-permute-start(bf16[64,12,2,896]{3,2,0,1:T(2,128)(2,1)} %copy.75), channel_id=1, source_target_pairs={{0,64},{64,0},{128,192},{192,128},{1,65},{65,1},{129,193},{193,129... | collective-permute-start | bytes 8257544 | tf_op jit(solution)/shard_map/ppermute | solution.py:8
  164.2 4.6 %copy-start.2 = (bf16[64,2,6,3584]{3,0,2,1:T(8,128)(2,1)S(1)}, bf16[64,2,6,3584]{3,0,2,1:T(8,128)(2,1)}, u32[]{:S(2)}) copy-start(bf16[64,2,6,3584]{3,0,2,1:T(8,128)(2,1)} %reshape.150) | copy-start | bytes 16515076
  164.2 5.6 %copy-start.3 = (bf16[1,3584,2,256]{3,2,1,0:T(2,128)(2,1)S(1)}, bf16[1,3584,2,256]{3,2,1,0:T(2,128)(2,1)}, u32[]{:S(2)}) copy-start(bf16[1,3584,2,256]{3,2,1,0:T(2,128)(2,1)} %get-tuple-element.6) | copy-start | bytes 11010052
  169.7 2.0 copy-start.6
  202.7 5.5 %collective-permute-start.2 = (bf16[64,12,2,896]{3,0,2,1:T(8,128)(2,1)S(1)}, bf16[64,12,2,896]{3,0,2,1:T(8,128)(2,1)S(1)}, u32[]{:S(2)}, u32[]{:S(2)}) collective-permute-start(bf16[64,12,2,896]{3,0,2,1:T(8,128)(2,1)S(1)} %select_bitcast_fusion), channel_id=1, source_target_pairs={{0,64},{64,0},{128,192},{192,128},{1,65},{65,1},{129,193},{193,129... | collective-permute-start | bytes 8257544 | tf_op jit(solution)/shard_map/ppermute | solution.py:8
  215.9 6.3 %copy-start.5 = (f32[64,8]{0,1:T(8,128)S(1)}, f32[64,8]{0,1:T(8,128)}, u32[]{:S(2)}) copy-start(f32[64,8]{0,1:T(8,128)} %param.8) | copy-start | bytes 6148
  215.9 90.7 %all-to-all-start.1 = ((bf16[64,12,1792]{2,1,0:T(8,128)(2,1)}), bf16[64,12,1792]{2,1,0:T(8,128)(2,1)}, u32[]{:S(2)}, u32[]{:S(2)}) async-start(bf16[64,12,1792]{2,1,0:T(8,128)(2,1)} %reshape.189), calls=%async_computation.1 | async-start | bytes 7340032 | tf_op jit(solution)/shard_map/all_to_all | solution.py:81
  312.0 20.8 %copy-start.1 = (s32[64,2]{0,1:T(2,128)S(1)}, s32[64,2]{0,1:T(2,128)}, u32[]{:S(2)}) copy-start(s32[64,2]{0,1:T(2,128)} %param.9) | copy-start | bytes 1540
  318.0 14.1 %collective-permute-start.3 = (f32[64,896]{1,0:T(8,128)S(1)}, f32[64,896]{1,0:T(8,128)S(1)}, u32[]{:S(2)}, u32[]{:S(2)}) collective-permute-start(f32[64,896]{1,0:T(8,128)S(1)} %select_bitcast_fusion.1), channel_id=1, source_target_pairs={{0,128},{64,192},{128,0},{192,64},{1,129},{65,193},{129,1},{193,65... | collective-permute-start | bytes 688136 | tf_op jit(solution)/shard_map/ppermute | solution.py:8

commit v2 on v1

v2 whole, which is shorter than its diff:
```python
import jax
import jax.numpy as jnp
import numpy as np
from jax import lax
from jax.sharding import Mesh
from jax.sharding import PartitionSpec as P

EP_AXES = ("z", "y", "x")
PLANE = ("y", "x")


def pair_swap(value, axis, bit):
    return lax.ppermute(value, axis, [(i, i ^ 1 << bit) for i in range(lax.axis_size(axis))])


def pick(flag, first, second):
    return jnp.where(flag, first, second), jnp.where(flag, second, first)


def holder_of(swap_plan, exp_dev):
    ep_size = swap_plan.shape[0]
    slot = jnp.arange(ep_size * exp_dev, dtype=jnp.int32)
    index = slot // exp_dev
    partner = swap_plan[index, 0]
    given = swap_plan[index, 1]
    moved = (partner != index) & (slot % exp_dev == given)
    return jnp.where(moved, partner * exp_dev + swap_plan[partner, 1], slot)


def shards(tokens, route_ids, route_weights, swap_plan, gate_up, down):
    n_z = lax.axis_size("z")
    n_plane = lax.axis_size("y") * lax.axis_size("x")
    ep_size = n_z * n_plane
    rep = lax.axis_index("rep")
    core = rep % 2
    half = rep // 2
    exp_dev = gate_up.shape[0]
    experts = exp_dev * ep_size
    tok_dev, top_k = route_ids.shape
    routed = tok_dev * top_k
    capacity = max(2, (routed * 3 + 2 * experts - 1) // (2 * experts))
    places = experts * capacity
    width = tokens.shape[1]
    cut = [slice(i * width, (i + 1) * width) for i in range(4)]

    holder = holder_of(swap_plan, exp_dev)
    owners = holder[route_ids.reshape(routed)]
    catalog = jnp.arange(experts, dtype=jnp.int32)
    one_hot = (owners[:, None] == catalog[None, :]).astype(jnp.float32)
    earlier = (jnp.arange(routed)[:, None] > jnp.arange(routed)[None, :]).astype(jnp.float32)
    before = jnp.dot(earlier, one_hot, preferred_element_type=jnp.float32)
    position = jnp.sum(before * one_hot, axis=1).astype(jnp.int32)
    device = owners // exp_dev
    group = (device % n_plane) * n_z + device // n_plane
    place = (group * exp_dev + owners % exp_dev) * capacity + position
    hits = (place[:, None] == jnp.arange(places, dtype=jnp.int32)[None, :]).reshape(tok_dev, top_k, places)
    gather = jnp.sum(hits.astype(jnp.bfloat16), axis=1)
    mixing = jnp.sum(jnp.where(hits, route_weights[:, :, None], 0.0), axis=1)

    other = pair_swap(tokens, "rep", 1)
    low, high = pick(half == 0, tokens, other)
    features = jnp.concatenate([low, high], axis=1)
    outgoing = lax.dot_general(
        gather, features, (((0,), (0,)), ((), ())), preferred_element_type=jnp.float32
    ).astype(jnp.bfloat16)

    step = lax.all_to_all(
        outgoing.reshape(n_plane, places // n_plane, 2 * width), PLANE, 0, 0, tiled=True
    )
    step = step.reshape(n_plane, n_z, exp_dev, capacity, 2 * width).transpose(1, 2, 0, 3, 4)
    mine = lax.all_to_all(
        step.reshape(n_z, places // n_z, 2 * width), "z", 0, 0, tiled=True
    ).reshape(n_z, exp_dev, n_plane * capacity, 2 * width)

    theirs = pair_swap(mine, "rep", 0)
    even, odd = pick(core == 0, mine, theirs)

    results = []
    for index in range(exp_dev):
        first = even[:, index]
        second = odd[:, index]
        rows = jnp.concatenate(
            [first[..., : width], second[..., : width], first[..., width:], second[..., width:]], axis=-1
        )
        projected = jnp.einsum(
            "zrd,dgf->zrgf", rows, gate_up[index], preferred_element_type=jnp.float32
        )
        hidden = (jax.nn.silu(projected[:, :, 0]) * projected[:, :, 1]).astype(jnp.bfloat16)
        results.append(
            jnp.einsum(
                "zrf,fd->zrd", hidden, down[index], preferred_element_type=jnp.float32
            ).astype(jnp.bfloat16)
        )
    partial = jnp.stack(results, axis=1)

    part_even = jnp.concatenate([partial[..., cut[0]], partial[..., cut[2]]], axis=-1)
    part_odd = jnp.concatenate([partial[..., cut[1]], partial[..., cut[3]]], axis=-1)
    keep, send = pick(core == 0, part_even, part_odd)
    paired = (keep.astype(jnp.float32) + pair_swap(send, "rep", 0).astype(jnp.float32)).astype(
        jnp.bfloat16
    )

    back = lax.all_to_all(paired.reshape(n_z, places // n_z, 2 * width), "z", 0, 0, tiled=True)
    back = back.reshape(n_z, exp_dev, n_plane, capacity, 2 * width).transpose(2, 0, 1, 3, 4)
    returned = lax.all_to_all(
        back.reshape(n_plane, places // n_plane, 2 * width), PLANE, 0, 0, tiled=True
    )
    weighted = jnp.dot(
        mixing,
        returned.reshape(places, 2 * width).astype(jnp.float32),
        precision=lax.Precision.HIGHEST,
        preferred_element_type=jnp.float32,
    )
    own, away = pick(half == 0, weighted[:, :width], weighted[:, width:])
    return (own + pair_swap(away, "rep", 1)).astype(jnp.bfloat16)


def solution(mesh):
    rep_size, ep_size = mesh.devices.shape
    side = round(ep_size ** (1 / 3))
    grid = Mesh(np.asarray(mesh.devices).reshape(rep_size, side, side, side), ("rep",) + EP_AXES)
    return jax.shard_map(
        shards,
        mesh=grid,
        in_specs=(
            P(EP_AXES, "rep"),
            P(EP_AXES, None),
            P(EP_AXES, None),
            P(),
            P(EP_AXES, None, None, "rep"),
            P(EP_AXES, "rep", None),
        ),
        out_specs=P(EP_AXES, "rep"),
        check_vma=False,
    )
```

time: 334 us -> 282 us (0.84)
  blocking collectives: 93.2 us -> 170 us
  local copies, waits for them, and re-layouts: 88.6 us -> 26.7 us
  waiting for transfers between devices: 101 us -> 51.7 us
  other arithmetic: 21.9 us -> 6.44 us
  matrix products: 11.8 us -> 7.73 us
    all_to_all x1 -> x3, blocking collectives: 93.2 us -> 170 us  [the longest x1 65.6 us: shards(): lax.all_to_all(paired.reshape(n_z, places // n_z, 2 * width), 'z', 0, 0,...]
    all_to_all x1, waiting for transfers between devices: 83.8 us -> 35.2 us  [shards(): lax.all_to_all(back.reshape(n_plane, places // n_plane, 2 * width), PLANE...]
    reshape x9 -> x3, local copies, waits for them, and re-layouts: 48.1 us -> 4.32 us  [the longest x1 2.34 us: shards(): back.reshape(n_plane, places // n_plane, 2 * width)]
    another operation x4 -> x1, other arithmetic: 17.8 us -> 0.56 us  [shards(): partial = jnp.stack(results, axis=1)]
    slice x1 -> x4, local copies, waits for them, and re-layouts: 13.6 us -> 0.45 us  [the longest x2 0.22 us: shards(): first[..., :width]]
    another operation x1 -> x0, local copies, waits for them, and re-layouts: 5.61 us -> none  [shards(): jnp.stack([first, second], axis=3)]
    dot_general x1 -> x0, local copies, waits for them, and re-layouts: 3.34 us -> none  [shards(): jnp.dot(mixing, returned.reshape(places, 2 * width).astype(jnp.float32),...]
  transfers between devices with their start and end apart: 5 -> 5, of which waited for: 3 -> 3; matrix products, arithmetic and copies ran while one was open for 5% -> 6% of each run, Pallas kernels for 0% -> 0%
where the time goes in v2:
time: 282 us; the launch traced here: 277 us
  blocking collectives  170 us (60%)
  waiting for transfers between devices  51.7 us (18%)
  local copies, waits for them, and re-layouts  26.7 us (9%)
  starting transfers between devices  14.5 us (5%)
  matrix products  7.73 us (3%)
  other arithmetic  6.44 us (2%)
    all_to_all x1, blocking collectives, shards(): lax.all_to_all(paired.reshape(n_z, places // n_z, 2 * width), 'z', 0, 0,...  65.6 us
    all_to_all x1, blocking collectives, shards(): lax.all_to_all(step.reshape(n_z, places // n_z, 2 * width), 'z', 0, 0, ti...  63.5 us
    all_to_all x1, blocking collectives, shards(): lax.all_to_all(outgoing.reshape(n_plane, places // n_plane, 2 * width), P...  41 us
    all_to_all x1, waiting for transfers between devices, shards(): lax.all_to_all(back.reshape(n_plane, places // n_plane, 2 * width), PLANE...  35.2 us
    ppermute x4, waiting for transfers between devices, pair_swap(): lax.ppermute(value, axis, [(i, i ^ 1 << bit) for i in range(lax.axis_size...  16.4 us
    ppermute x4, starting transfers between devices, pair_swap(): lax.ppermute(value, axis, [(i, i ^ 1 << bit) for i in range(lax.axis_size...  9.37 us
    slice x1, local copies, waits for them, and re-layouts, shards(): gate_up[index]  6.37 us
  transfers between devices with their start and end apart: 5, of which 3 were waited for; matrix products, arithmetic and copies ran while one was open for 6% of the time, Pallas kernels for 0%

profile of v2, /device:TPU:2, one launch (start us, length us, event | category | flops | bytes accessed | tf_op | source)
XLA Modules:
  0.0 277.5 jit_solution(7789691789515323834)
XLA Ops:
  0.0 7.2 %collective-permute-start = (bf16[64,896]{1,0:T(8,128)(2,1)}, bf16[64,896]{1,0:T(8,128)(2,1)S(1)}, u32[]{:S(2)}, u32[]{:S(2)}) collective-permute-start(bf16[64,896]{1,0:T(8,128)(2,1)} %param.6), channel_id=1, source_target_pairs={{0,128},{64,192},{128,0},{192,64},{1,129},{65,193},{129,1},{193,65... | collective-permute-start | bytes 344072 | tf_op jit(solution)/shard_map/ppermute | solution.py:13
  7.2 1.5 gather_fusion
  8.8 1.5 gather_fusion.2
  10.3 1.5 gather_fusion.1
  11.8 0.8 copy.51
  12.6 0.1 reshape.190
  12.7 3.3 %gather_fusion.3 = s32[512]{0:T(512)S(1)} fusion(s32[128]{0:T(128)S(1)} %and_select_fusion, s32[1024]{0:T(1024)S(1)} %pad_clamp_fusion), kind=kCustom, calls=%fused_computation.3 | custom fusion | bytes 6144 | tf_op jit(solution)/shard_map/gather | solution.py:47
  16.1 0.3 fusion.28
  16.4 0.1 gather.21
  16.5 0.1 convert_element_type.52
  16.7 0.5 fusion.29
  17.2 0.9 convolution_convert_fusion.2
  18.2 41.0 %all_to_all.20 = bf16[16,48,1792]{2,1,0:T(8,128)(2,1)S(1)} all-to-all(bf16[16,48,1792]{2,1,0:T(8,128)(2,1)S(1)} %bitcast.71), channel_id=1, replica_groups=mesh['rep'=4,'z'=4,'y'=4,'x'=4] {'y','x'}, dimensions={0} | all-to-all | bytes 5505024 | tf_op jit(solution)/shard_map/all_to_all | solution.py:67
  59.2 0.8 copy.53
  60.0 2.1 copy.54
  62.1 0.3 copy.55
  62.4 63.5 %all_to_all.21 = bf16[4,192,1792]{2,1,0:T(8,128)(2,1)S(1)} all-to-all(bf16[4,192,1792]{2,1,0:T(8,128)(2,1)S(1)} %copy.55), channel_id=1, replica_groups=mesh['rep'=4,'z'=4,'y'=4,'x'=4] {'z'}, dimensions={0} | all-to-all | bytes 5505024 | tf_op jit(solution)/shard_map/all_to_all | solution.py:71
  125.9 1.7 copy.57
  127.6 6.4 %fusion.64 = (bf16[1,3584,2,256]{3,2,1,0:T(2,128)(2,1)S(1)}, bf16[1,3584,2,256]{3,2,1,0:T(2,128)(2,1)S(1)}) fusion(bf16[2,3584,2,256]{3,2,1,0:T(2,128)(2,1)} %param.10), kind=kLoop, calls=%fused_computation.127 | loop fusion | bytes 14680064 | tf_op jit(solution)/shard_map/slice | solution.py:86
  134.0 2.1 broadcast_select_fusion.2
  136.2 0.4 slice_bitcast_fusion
  136.6 0.1 fusion.65
  136.7 0.1 fusion.66
  136.8 0.1 fusion.67
  137.0 0.1 fusion.68
  137.1 1.6 fusion.4
  138.7 0.4 copy-done.4
  139.1 0.9 fusion.3
  140.0 1.6 fusion.5
  141.6 0.9 fusion.2
  142.6 0.6 fusion.25
  143.1 0.7 broadcast_select_fusion
  143.8 0.6 collective-permute-start.2
  144.4 4.7 %collective-permute-done.2 = bf16[4,2,96,1792]{3,2,0,1:T(8,128)(2,1)S(1)} collective-permute-done((bf16[4,2,96,1792]{3,2,0,1:T(8,128)(2,1)S(1)}, bf16[4,2,96,1792]{3,2,0,1:T(8,128)(2,1)S(1)}, u32[]{:S(2)}, u32[]{:S(2)}) %collective-permute-start.2) | collective-permute-done | bytes 2752544 | tf_op jit(solution)/shard_map/ppermute | solution.py:13
  149.2 1.1 add_convert_fusion
  150.2 0.2 copy.61
  150.4 65.6 %all_to_all.22 = bf16[4,192,1792]{2,1,0:T(8,128)(2,1)S(1)} all-to-all(bf16[4,192,1792]{2,1,0:T(8,128)(2,1)S(1)} %bitcast.74), channel_id=1, replica_groups=mesh['rep'=4,'z'=4,'y'=4,'x'=4] {'z'}, dimensions={0} | all-to-all | bytes 5505024 | tf_op jit(solution)/shard_map/all_to_all | solution.py:103
  216.0 2.1 copy.62
  218.1 0.5 copy.63
  218.6 2.3 copy.64
  220.9 5.1 %all-to-all-start.3 = ((bf16[16,48,1792]{2,1,0:T(8,128)(2,1)}), bf16[16,48,1792]{2,1,0:T(8,128)(2,1)S(1)}, u32[]{:S(2)}, u32[]{:S(2)}) async-start(bf16[16,48,1792]{2,1,0:T(8,128)(2,1)} %copy.64), calls=%async_computation.3 | async-start | bytes 5505024 | tf_op jit(solution)/shard_map/all_to_all | solution.py:105
  226.1 0.1 copy.52
  226.2 0.5 select_reduce_fusion
  226.7 35.2 %all-to-all-done.3 = bf16[16,48,1792]{2,1,0:T(8,128)(2,1)S(1)} async-done(((bf16[16,48,1792]{2,1,0:T(8,128)(2,1)}), bf16[16,48,1792]{2,1,0:T(8,128)(2,1)S(1)}, u32[]{:S(2)}, u32[]{:S(2)}) %all-to-all-start.3) | async-done | bytes 2752544 | tf_op jit(solution)/shard_map/all_to_all | solution.py:105
  261.9 1.5 fusion.69
  263.5 1.6 collective-permute-start.3
  265.1 11.7 %collective-permute-done.3 = f32[64,896]{1,0:T(8,128)S(1)} collective-permute-done((f32[64,896]{1,0:T(8,128)S(1)}, f32[64,896]{1,0:T(8,128)S(1)}, u32[]{:S(2)}, u32[]{:S(2)}) %collective-permute-start.3) | collective-permute-done | bytes 229408 | tf_op jit(solution)/shard_map/ppermute | solution.py:13
  276.8 0.7 add_convert_fusion.1
  (22 shorter events, 0.2 us)
Async XLA Ops:
  0.0 7.2 %copy-start = (s32[64,2]{0,1:T(2,128)S(1)}, s32[64,2]{0,1:T(2,128)}, u32[]{:S(2)}) copy-start(s32[64,2]{0,1:T(2,128)} %param.9) | copy-start | bytes 1540
  0.0 17.2 %copy-start.2 = (bf16[64,896]{1,0:T(8,128)(2,1)S(1)}, bf16[64,896]{1,0:T(8,128)(2,1)}, u32[]{:S(2)}) copy-start(bf16[64,896]{1,0:T(8,128)(2,1)} %param.6) | copy-start | bytes 344068
  0.0 17.2 %collective-permute-start = (bf16[64,896]{1,0:T(8,128)(2,1)}, bf16[64,896]{1,0:T(8,128)(2,1)S(1)}, u32[]{:S(2)}, u32[]{:S(2)}) collective-permute-start(bf16[64,896]{1,0:T(8,128)(2,1)} %param.6), channel_id=1, source_target_pairs={{0,128},{64,192},{128,0},{192,64},{1,129},{65,193},{129,1},{193,65... | collective-permute-start | bytes 344072 | tf_op jit(solution)/shard_map/ppermute | solution.py:13
  127.6 6.4 %collective-permute-start.1 = (bf16[4,2,96,1792]{3,2,0,1:T(8,128)(2,1)}, bf16[4,2,96,1792]{3,2,0,1:T(8,128)(2,1)}, u32[]{:S(2)}, u32[]{:S(2)}) collective-permute-start(bf16[4,2,96,1792]{3,2,0,1:T(8,128)(2,1)} %copy.57), channel_id=1, source_target_pairs={{0,64},{64,0},{128,192},{192,128},{1,65},{65,1},{129,193},{193,129... | collective-permute-start | bytes 8257544 | tf_op jit(solution)/shard_map/ppermute | solution.py:13
  137.1 2.0 copy-start.4
  143.8 5.3 %collective-permute-start.2 = (bf16[4,2,96,1792]{3,2,0,1:T(8,128)(2,1)S(1)}, bf16[4,2,96,1792]{3,2,0,1:T(8,128)(2,1)S(1)}, u32[]{:S(2)}, u32[]{:S(2)}) collective-permute-start(bf16[4,2,96,1792]{3,2,0,1:T(8,128)(2,1)S(1)} %broadcast_select_fusion), channel_id=1, source_target_pairs={{0,64},{64,0},{128,192},{192,128},{1,65},{65,1},{129,193},{193,129... | collective-permute-start | bytes 8257544 | tf_op jit(solution)/shard_map/ppermute | solution.py:13
  220.9 5.1 %copy-start.3 = (f32[64,8]{0,1:T(8,128)S(1)}, f32[64,8]{0,1:T(8,128)}, u32[]{:S(2)}) copy-start(f32[64,8]{0,1:T(8,128)} %param.8) | copy-start | bytes 6148
  220.9 41.0 %all-to-all-start.3 = ((bf16[16,48,1792]{2,1,0:T(8,128)(2,1)}), bf16[16,48,1792]{2,1,0:T(8,128)(2,1)S(1)}, u32[]{:S(2)}, u32[]{:S(2)}) async-start(bf16[16,48,1792]{2,1,0:T(8,128)(2,1)} %copy.64), calls=%async_computation.3 | async-start | bytes 5505024 | tf_op jit(solution)/shard_map/all_to_all | solution.py:105
  226.1 51.4 %copy-start.1 = (s32[64,2]{0,1:T(2,128)S(1)}, s32[64,2]{0,1:T(2,128)}, u32[]{:S(2)}) copy-start(s32[64,2]{0,1:T(2,128)} %param.9) | copy-start | bytes 1540
  263.5 13.3 %collective-permute-start.3 = (f32[64,896]{1,0:T(8,128)S(1)}, f32[64,896]{1,0:T(8,128)S(1)}, u32[]{:S(2)}, u32[]{:S(2)}) collective-permute-start(f32[64,896]{1,0:T(8,128)S(1)} %slice_select_fusion), channel_id=1, source_target_pairs={{0,128},{64,192},{128,0},{192,64},{1,129},{65,193},{129,1},{193,65... | collective-permute-start | bytes 688136 | tf_op jit(solution)/shard_map/ppermute | solution.py:13

commit v3 on v2

--- a/solution.py
+++ b/solution.py
@@ -6,11 +6,18 @@
 from jax.sharding import PartitionSpec as P
 
 EP_AXES = ("z", "y", "x")
+REP_AXES = ("zh", "core")
+RING = ("zh", "z")
 PLANE = ("y", "x")
 
 
-def pair_swap(value, axis, bit):
-    return lax.ppermute(value, axis, [(i, i ^ 1 << bit) for i in range(lax.axis_size(axis))])
+def pair_swap(value, axis):
+    return lax.ppermute(value, axis, [(0, 1), (1, 0)])
+
+
+def ring_shift(value, shift):
+    size = lax.axis_size(RING)
+    return lax.ppermute(value, RING, [(i, (i + shift) % size) for i in range(size)])
 
 
 def pick(flag, first, second):
@@ -31,9 +38,8 @@
     n_z = lax.axis_size("z")
     n_plane = lax.axis_size("y") * lax.axis_size("x")
     ep_size = n_z * n_plane
-    rep = lax.axis_index("rep")
-    core = rep % 2
-    half = rep // 2
+    core = lax.axis_index("core")
+    half = lax.axis_index("zh")
     exp_dev = gate_up.shape[0]
     experts = exp_dev * ep_size
     tok_dev, top_k = route_ids.shape
@@ -51,13 +57,14 @@
     before = jnp.dot(earlier, one_hot, preferred_element_type=jnp.float32)
     position = jnp.sum(before * one_hot, axis=1).astype(jnp.int32)
     device = owners // exp_dev
-    group = (device % n_plane) * n_z + device // n_plane
+    offset = (device // n_plane - lax.axis_index("z")) % n_z
+    group = (device % n_plane) * n_z + offset
     place = (group * exp_dev + owners % exp_dev) * capacity + position
     hits = (place[:, None] == jnp.arange(places, dtype=jnp.int32)[None, :]).reshape(tok_dev, top_k, places)
     gather = jnp.sum(hits.astype(jnp.bfloat16), axis=1)
     mixing = jnp.sum(jnp.where(hits, route_weights[:, :, None], 0.0), axis=1)
 
-    other = pair_swap(tokens, "rep", 1)
+    other = pair_swap(tokens, "zh")
     low, high = pick(half == 0, tokens, other)
     features = jnp.concatenate([low, high], axis=1)
     outgoing = lax.dot_general(
@@ -68,11 +75,13 @@
         outgoing.reshape(n_plane, places // n_plane, 2 * width), PLANE, 0, 0, tiled=True
     )
     step = step.reshape(n_plane, n_z, exp_dev, capacity, 2 * width).transpose(1, 2, 0, 3, 4)
-    mine = lax.all_to_all(
-        step.reshape(n_z, places // n_z, 2 * width), "z", 0, 0, tiled=True
-    ).reshape(n_z, exp_dev, n_plane * capacity, 2 * width)
+    step = step.reshape(n_z, exp_dev, n_plane * capacity, 2 * width)
+    far = jnp.concatenate(
+        [ring_shift(step[2, :1], 2), ring_shift(step[2, 1:], -2)], axis=0
+    )
+    mine = jnp.stack([step[0], ring_shift(step[1], 1), far, ring_shift(step[3], -1)])
 
-    theirs = pair_swap(mine, "rep", 0)
+    theirs = pair_swap(mine, "core")
     even, odd = pick(core == 0, mine, theirs)
 
     results = []
@@ -96,11 +105,14 @@
     part_even = jnp.concatenate([partial[..., cut[0]], partial[..., cut[2]]], axis=-1)
     part_odd = jnp.concatenate([partial[..., cut[1]], partial[..., cut[3]]], axis=-1)
     keep, send = pick(core == 0, part_even, part_odd)
-    paired = (keep.astype(jnp.float32) + pair_swap(send, "rep", 0).astype(jnp.float32)).astype(
+    paired = (keep.astype(jnp.float32) + pair_swap(send, "core").astype(jnp.float32)).astype(
         jnp.bfloat16
     )
 
-    back = lax.all_to_all(paired.reshape(n_z, places // n_z, 2 * width), "z", 0, 0, tiled=True)
+    far = jnp.concatenate(
+        [ring_shift(paired[2, :1], -2), ring_shift(paired[2, 1:], 2)], axis=0
+    )
+    back = jnp.stack([paired[0], ring_shift(paired[1], -1), far, ring_shift(paired[3], 1)])
     back = back.reshape(n_z, exp_dev, n_plane, capacity, 2 * width).transpose(2, 0, 1, 3, 4)
     returned = lax.all_to_all(
         back.reshape(n_plane, places // n_plane, 2 * width), PLANE, 0, 0, tiled=True
@@ -112,24 +124,25 @@
         preferred_element_type=jnp.float32,
     )
     own, away = pick(half == 0, weighted[:, :width], weighted[:, width:])
-    return (own + pair_swap(away, "rep", 1)).astype(jnp.bfloat16)
+    return (own + pair_swap(away, "zh")).astype(jnp.bfloat16)
 
 
 def solution(mesh):
     rep_size, ep_size = mesh.devices.shape
     side = round(ep_size ** (1 / 3))
-    grid = Mesh(np.asarray(mesh.devices).reshape(rep_size, side, side, side), ("rep",) + EP_AXES)
+    shape = (2, rep_size // 2, side, side, side)
+    grid = Mesh(np.asarray(mesh.devices).reshape(shape), REP_AXES + EP_AXES)
     return jax.shard_map(
         shards,
         mesh=grid,
         in_specs=(
-            P(EP_AXES, "rep"),
+            P(EP_AXES, REP_AXES),
             P(EP_AXES, None),
             P(EP_AXES, None),
             P(),
-            P(EP_AXES, None, None, "rep"),
-            P(EP_AXES, "rep", None),
+            P(EP_AXES, None, None, REP_AXES),
+            P(EP_AXES, REP_AXES, None),
         ),
-        out_specs=P(EP_AXES, "rep"),
+        out_specs=P(EP_AXES, REP_AXES),
         check_vma=False,
     )

time: 282 us -> 229 us (0.81)
  the two profiles are of different devices: /device:TPU:2 before, /device:TPU:33 now
where the time goes in v3:
time: 229 us; the launch traced here: 228 us
  waiting for transfers between devices  110 us (48%)
  blocking collectives  40.5 us (18%)
  local copies, waits for them, and re-layouts  29.5 us (13%)
  starting transfers between devices  26.4 us (12%)
  other arithmetic  13.4 us (6%)
  matrix products  7.7 us (3%)
    ppermute x8, waiting for transfers between devices, ring_shift(): lax.ppermute(value, RING, [(i, (i + shift) % size) for i in range(size)])  52.1 us
    all_to_all x1, blocking collectives, shards(): lax.all_to_all(outgoing.reshape(n_plane, places // n_plane, 2 * width), P...  40.5 us
    all_to_all x1, waiting for transfers between devices, shards(): lax.all_to_all(back.reshape(n_plane, places // n_plane, 2 * width), PLANE...  40.1 us
    ppermute x4, waiting for transfers between devices, pair_swap(): return lax.ppermute(value, axis, [(0, 1), (1, 0)])  18.2 us
    ppermute x4, starting transfers between devices, pair_swap(): return lax.ppermute(value, axis, [(0, 1), (1, 0)])  11.7 us
    ppermute x8, starting transfers between devices, ring_shift(): lax.ppermute(value, RING, [(i, (i + shift) % size) for i in range(size)])  10.8 us
    slice x1, local copies, waits for them, and re-layouts, shards(): gate_up[index]  6.37 us
    transpose x1, other arithmetic, shards(): back.reshape(n_z, exp_dev, n_plane, capacity, 2 * width)  5.1 us
  transfers between devices with their start and end apart: 13, of which 6 were waited for; matrix products, arithmetic and copies ran while one was open for 10% of the time, Pallas kernels for 0%

profile of v3, /device:TPU:33, one launch (start us, length us, event | category | flops | bytes accessed | tf_op | source)
XLA Modules:
  0.0 228.3 jit_solution(17442457399995941012)
XLA Ops:
  0.0 6.0 %collective-permute-start = (bf16[64,896]{1,0:T(8,128)(2,1)}, bf16[64,896]{1,0:T(8,128)(2,1)S(1)}, u32[]{:S(2)}, u32[]{:S(2)}) collective-permute-start(bf16[64,896]{1,0:T(8,128)(2,1)} %param.6), channel_id=1, source_target_pairs={{0,128},{128,0},{1,129},{129,1},{2,130},{130,2},{3,131},{131,3},{4... | collective-permute-start | bytes 344072 | tf_op jit(solution)/shard_map/ppermute | solution.py:15
  6.1 1.5 gather_fusion
  7.6 1.5 gather_fusion.2
  9.1 1.5 gather_fusion.1
  10.6 0.8 copy.74
  11.5 3.3 %gather_fusion.3 = s32[512]{0:T(512)S(1)} fusion(s32[128]{0:T(128)S(1)} %and_select_fusion, s32[1024]{0:T(1024)S(1)} %pad_clamp_fusion), kind=kCustom, calls=%fused_computation.3 | custom fusion | bytes 6144 | tf_op jit(solution)/shard_map/gather | solution.py:53
  16.1 0.9 convolution_convert_fusion.2
  17.0 40.5 %all_to_all.10 = bf16[16,48,1792]{2,1,0:T(8,128)(2,1)S(1)} all-to-all(bf16[16,48,1792]{2,1,0:T(8,128)(2,1)S(1)} %bitcast.95), channel_id=1, replica_groups=mesh['zh'=2,'core'=2,'z'=4,'y'=4,'x'=4] {'y','x'}, dimensions={0} | all-to-all | bytes 5505024 | tf_op jit(solution)/shard_map/all_to_all | solution.py:74
  57.5 0.8 copy.76
  58.3 2.8 %copy.80 = bf16[4,2,16,6,1792]{4,1,3,2,0:T(2,128)(2,1)S(1)} copy(bf16[4,2,16,6,1792]{4,2,3,1,0:T(8,128)(2,1)S(1)} %bitcast.92) | data formatting | bytes 5505024 | tf_op jit(solution)/shard_map/transpose | solution.py:77
  61.3 0.7 copy.78
  62.1 0.8 collective-permute-start.1
  62.9 0.7 copy.83
  63.7 1.0 collective-permute-start.4
  64.7 1.0 fusion.66
  65.7 1.3 collective-permute-start.2
  67.0 2.4 %collective-permute-start.3 = (bf16[1,96,1792]{2,1,0:T(8,128)(2,1)S(1)}, bf16[1,96,1792]{2,1,0:T(8,128)(2,1)S(1)}, u32[]{:S(2)}, u32[]{:S(2)}) collective-permute-start(bf16[1,96,1792]{2,1,0:T(8,128)(2,1)S(1)} %bitcast.110), channel_id=1, source_target_pairs={{0,160},{16,176},{32,0},{48,16},{128,32},{144,48},{160,128},{176,1... | collective-permute-start | bytes 1032200 | tf_op jit(solution)/shard_map/ppermute | solution.py:20
  69.4 0.7 copy.77
  70.2 22.9 %collective-permute-done.2 = bf16[1,96,1792]{2,1,0:T(8,128)(2,1)S(1)} collective-permute-done((bf16[1,96,1792]{2,1,0:T(8,128)(2,1)S(1)}, bf16[1,96,1792]{2,1,0:T(8,128)(2,1)S(1)}, u32[]{:S(2)}, u32[]{:S(2)}) %collective-permute-start.2) | collective-permute-done | bytes 344096 | tf_op jit(solution)/shard_map/ppermute | solution.py:20
  93.2 1.7 pad_maximum_fusion
  94.9 3.3 %collective-permute-start.5 = (bf16[4,2,96,1792]{3,2,0,1:T(8,128)(2,1)}, bf16[4,2,96,1792]{3,2,0,1:T(8,128)(2,1)}, u32[]{:S(2)}, u32[]{:S(2)}) collective-permute-start(bf16[4,2,96,1792]{3,2,0,1:T(8,128)(2,1)} %pad_maximum_fusion), channel_id=1, source_target_pairs={{0,64},{64,0},{1,65},{65,1},{2,66},{66,2},{3,67},{67,3},{4,68},{68... | collective-permute-start | bytes 8257544 | tf_op jit(solution)/shard_map/ppermute | solution.py:15
  98.3 6.4 %fusion.63 = (bf16[1,3584,2,256]{3,2,1,0:T(2,128)(2,1)S(1)}, bf16[1,3584,2,256]{3,2,1,0:T(2,128)(2,1)S(1)}) fusion(bf16[2,3584,2,256]{3,2,1,0:T(2,128)(2,1)} %param.10), kind=kLoop, calls=%fused_computation.139 | loop fusion | bytes 14680064 | tf_op jit(solution)/shard_map/slice | solution.py:95
  104.6 2.1 broadcast_select_fusion.2
  107.7 1.6 fusion.4
  109.7 0.9 fusion.3
  110.6 1.6 fusion.5
  112.2 0.9 fusion.2
  113.1 0.6 fusion.25
  113.7 0.7 broadcast_select_fusion
  114.5 5.1 %collective-permute-done.6 = bf16[4,2,96,1792]{3,2,0,1:T(8,128)(2,1)S(1)} collective-permute-done((bf16[4,2,96,1792]{3,2,0,1:T(8,128)(2,1)S(1)}, bf16[4,2,96,1792]{3,2,0,1:T(8,128)(2,1)S(1)}, u32[]{:S(2)}, u32[]{:S(2)}) %collective-permute-start.6) | collective-permute-done | bytes 2752544 | tf_op jit(solution)/shard_map/ppermute | solution.py:15
  119.6 1.1 add_convert_fusion
  120.8 1.6 collective-permute-start.7
  122.4 0.6 collective-permute-start.10
  123.0 3.1 %collective-permute-start.8 = (bf16[1,96,1792]{2,1,0:T(8,128)(2,1)S(1)}, bf16[1,96,1792]{2,1,0:T(8,128)(2,1)S(1)}, u32[]{:S(2)}, u32[]{:S(2)}) collective-permute-start(bf16[1,96,1792]{2,1,0:T(8,128)(2,1)S(1)} %get-tuple-element.15), channel_id=1, source_target_pairs={{0,160},{16,176},{32,0},{48,16},{128,32},{144,48},{160,128},{176,1... | collective-permute-start | bytes 1032200 | tf_op jit(solution)/shard_map/ppermute | solution.py:20
  126.1 0.7 copy.88
  126.8 27.2 %collective-permute-done.8 = bf16[1,96,1792]{2,1,0:T(8,128)(2,1)S(1)} collective-permute-done((bf16[1,96,1792]{2,1,0:T(8,128)(2,1)S(1)}, bf16[1,96,1792]{2,1,0:T(8,128)(2,1)S(1)}, u32[]{:S(2)}, u32[]{:S(2)}) %collective-permute-start.8) | collective-permute-done | bytes 344096 | tf_op jit(solution)/shard_map/ppermute | solution.py:20
  154.0 2.0 collective-permute-done.9
  156.1 0.7 copy.91
  156.8 0.7 copy.89
  157.6 0.7 copy.92
  158.3 5.1 %maximum_bitcast_fusion.4 = bf16[16,4,2,6,1792]{4,2,3,0,1:T(2,128)(2,1)S(1)} fusion(bf16[1,2,16,6,1792]{4,1,3,2,0:T(2,128)(2,1)S(1)} %bitcast.104, bf16[1,2,16,6,1792]{4,1,3,2,0:T(2,128)(2,1)S(1)} %bitcast.102, bf16[1,2,16,6,1792]{4,1,3,2,0:T(2,128)(2,1)S(1)} %bitcast.103, bf16[1,2,16,6,1792]{4,1,3,2,0:T(2,128)(2,1)S(1)} %bitcast.101), kind=kLoop, calls=%fused_computation.41 | loop fusion | flops 4128768 | bytes 5505024 | tf_op jit(solution)/shard_map/transpose | solution.py:116
  163.7 2.3 %copy.94 = bf16[16,48,1792]{2,1,0:T(8,128)(2,1)} copy(bf16[16,48,1792]{2,0,1:T(8,128)(2,1)S(1)} %bitcast.96) | data formatting | bytes 5505024 | tf_op jit(solution)/shard_map/reshape | solution.py:118
  166.1 3.9 %all-to-all-start.1 = ((bf16[16,48,1792]{2,1,0:T(8,128)(2,1)}), bf16[16,48,1792]{2,1,0:T(8,128)(2,1)S(1)}, u32[]{:S(2)}, u32[]{:S(2)}) async-start(bf16[16,48,1792]{2,1,0:T(8,128)(2,1)} %copy.94), calls=%async_computation.1 | async-start | bytes 5505024 | tf_op jit(solution)/shard_map/all_to_all | solution.py:117
  170.6 40.1 %all-to-all-done.1 = bf16[16,48,1792]{2,1,0:T(8,128)(2,1)S(1)} async-done(((bf16[16,48,1792]{2,1,0:T(8,128)(2,1)}), bf16[16,48,1792]{2,1,0:T(8,128)(2,1)S(1)}, u32[]{:S(2)}, u32[]{:S(2)}) %all-to-all-start.1) | async-done | bytes 2752544 | tf_op jit(solution)/shard_map/all_to_all | solution.py:117
  210.7 1.5 fusion.71
  212.2 2.3 %collective-permute-start.11 = (f32[64,896]{1,0:T(8,128)S(1)}, f32[64,896]{1,0:T(8,128)S(1)}, u32[]{:S(2)}, u32[]{:S(2)}) collective-permute-start(f32[64,896]{1,0:T(8,128)S(1)} %slice_select_fusion), channel_id=1, source_target_pairs={{0,128},{128,0},{1,129},{129,1},{2,130},{130,2},{3,131},{131,3},{4... | collective-permute-start | bytes 688136 | tf_op jit(solution)/shard_map/ppermute | solution.py:15
  214.5 13.1 %collective-permute-done.11 = f32[64,896]{1,0:T(8,128)S(1)} collective-permute-done((f32[64,896]{1,0:T(8,128)S(1)}, f32[64,896]{1,0:T(8,128)S(1)}, u32[]{:S(2)}, u32[]{:S(2)}) %collective-permute-start.11) | collective-permute-done | bytes 229408 | tf_op jit(solution)/shard_map/ppermute | solution.py:15
  227.6 0.7 add_convert_fusion.1
  (52 shorter events, 4.4 us)
Async XLA Ops:
  0.0 6.0 %copy-start = (s32[64,2]{0,1:T(2,128)S(1)}, s32[64,2]{0,1:T(2,128)}, u32[]{:S(2)}) copy-start(s32[64,2]{0,1:T(2,128)} %param.9) | copy-start | bytes 1540
  0.0 16.0 %copy-start.2 = (bf16[64,896]{1,0:T(8,128)(2,1)S(1)}, bf16[64,896]{1,0:T(8,128)(2,1)}, u32[]{:S(2)}) copy-start(bf16[64,896]{1,0:T(8,128)(2,1)} %param.6) | copy-start | bytes 344068
  0.0 16.0 %collective-permute-start = (bf16[64,896]{1,0:T(8,128)(2,1)}, bf16[64,896]{1,0:T(8,128)(2,1)S(1)}, u32[]{:S(2)}, u32[]{:S(2)}) collective-permute-start(bf16[64,896]{1,0:T(8,128)(2,1)} %param.6), channel_id=1, source_target_pairs={{0,128},{128,0},{1,129},{129,1},{2,130},{130,2},{3,131},{131,3},{4... | collective-permute-start | bytes 344072 | tf_op jit(solution)/shard_map/ppermute | solution.py:15
  62.1 31.1 %collective-permute-start.1 = (bf16[2,96,1792]{2,1,0:T(8,128)(2,1)S(1)}, bf16[2,96,1792]{2,1,0:T(8,128)(2,1)S(1)}, u32[]{:S(2)}, u32[]{:S(2)}) collective-permute-start(bf16[2,96,1792]{2,1,0:T(8,128)(2,1)S(1)} %copy.79), channel_id=1, source_target_pairs={{0,16},{16,32},{32,48},{48,128},{128,144},{144,160},{160,176},{176... | collective-permute-start | bytes 2064392 | tf_op jit(solution)/shard_map/ppermute | solution.py:20
  63.7 29.5 %collective-permute-start.4 = (bf16[2,96,1792]{2,1,0:T(8,128)(2,1)S(1)}, bf16[2,96,1792]{2,1,0:T(8,128)(2,1)S(1)}, u32[]{:S(2)}, u32[]{:S(2)}) collective-permute-start(bf16[2,96,1792]{2,1,0:T(8,128)(2,1)S(1)} %copy.84), channel_id=1, source_target_pairs={{0,176},{16,0},{32,16},{48,32},{128,48},{144,128},{160,144},{176,1... | collective-permute-start | bytes 2064392 | tf_op jit(solution)/shard_map/ppermute | solution.py:20
  65.7 27.4 %collective-permute-start.2 = (bf16[1,96,1792]{2,1,0:T(8,128)(2,1)S(1)}, bf16[1,96,1792]{2,1,0:T(8,128)(2,1)S(1)}, u32[]{:S(2)}, u32[]{:S(2)}) collective-permute-start(bf16[1,96,1792]{2,1,0:T(8,128)(2,1)S(1)} %bitcast.109), channel_id=1, source_target_pairs={{0,32},{16,48},{32,128},{48,144},{128,160},{144,176},{160,0},{176,... | collective-permute-start | bytes 1032200 | tf_op jit(solution)/shard_map/ppermute | solution.py:20
  67.0 26.1 %collective-permute-start.3 = (bf16[1,96,1792]{2,1,0:T(8,128)(2,1)S(1)}, bf16[1,96,1792]{2,1,0:T(8,128)(2,1)S(1)}, u32[]{:S(2)}, u32[]{:S(2)}) collective-permute-start(bf16[1,96,1792]{2,1,0:T(8,128)(2,1)S(1)} %bitcast.110), channel_id=1, source_target_pairs={{0,160},{16,176},{32,0},{48,16},{128,32},{144,48},{160,128},{176,1... | collective-permute-start | bytes 1032200 | tf_op jit(solution)/shard_map/ppermute | solution.py:20
  94.9 9.7 %collective-permute-start.5 = (bf16[4,2,96,1792]{3,2,0,1:T(8,128)(2,1)}, bf16[4,2,96,1792]{3,2,0,1:T(8,128)(2,1)}, u32[]{:S(2)}, u32[]{:S(2)}) collective-permute-start(bf16[4,2,96,1792]{3,2,0,1:T(8,128)(2,1)} %pad_maximum_fusion), channel_id=1, source_target_pairs={{0,64},{64,0},{1,65},{65,1},{2,66},{66,2},{3,67},{67,3},{4,68},{68... | collective-permute-start | bytes 8257544 | tf_op jit(solution)/shard_map/ppermute | solution.py:15
  107.7 2.0 copy-start.4
  114.4 5.2 %collective-permute-start.6 = (bf16[4,2,96,1792]{3,2,0,1:T(8,128)(2,1)S(1)}, bf16[4,2,96,1792]{3,2,0,1:T(8,128)(2,1)S(1)}, u32[]{:S(2)}, u32[]{:S(2)}) collective-permute-start(bf16[4,2,96,1792]{3,2,0,1:T(8,128)(2,1)S(1)} %broadcast_select_fusion), channel_id=1, source_target_pairs={{0,64},{64,0},{1,65},{65,1},{2,66},{66,2},{3,67},{67,3},{4,68},{68... | collective-permute-start | bytes 8257544 | tf_op jit(solution)/shard_map/ppermute | solution.py:15
  120.8 36.0 %collective-permute-start.7 = (bf16[2,96,1792]{2,1,0:T(8,128)(2,1)S(1)}, bf16[2,96,1792]{2,1,0:T(8,128)(2,1)S(1)}, u32[]{:S(2)}, u32[]{:S(2)}) collective-permute-start(bf16[2,96,1792]{2,1,0:T(8,128)(2,1)S(1)} %get-tuple-element.14), channel_id=1, source_target_pairs={{0,176},{16,0},{32,16},{48,32},{128,48},{144,128},{160,144},{176,1... | collective-permute-start | bytes 2064392 | tf_op jit(solution)/shard_map/ppermute | solution.py:20
  122.4 35.2 %collective-permute-start.10 = (bf16[2,96,1792]{2,1,0:T(8,128)(2,1)S(1)}, bf16[2,96,1792]{2,1,0:T(8,128)(2,1)S(1)}, u32[]{:S(2)}, u32[]{:S(2)}) collective-permute-start(bf16[2,96,1792]{2,1,0:T(8,128)(2,1)S(1)} %get-tuple-element.13), channel_id=1, source_target_pairs={{0,16},{16,32},{32,48},{48,128},{128,144},{144,160},{160,176},{176... | collective-permute-start | bytes 2064392 | tf_op jit(solution)/shard_map/ppermute | solution.py:20
  123.0 31.0 %collective-permute-start.8 = (bf16[1,96,1792]{2,1,0:T(8,128)(2,1)S(1)}, bf16[1,96,1792]{2,1,0:T(8,128)(2,1)S(1)}, u32[]{:S(2)}, u32[]{:S(2)}) collective-permute-start(bf16[1,96,1792]{2,1,0:T(8,128)(2,1)S(1)} %get-tuple-element.15), channel_id=1, source_target_pairs={{0,160},{16,176},{32,0},{48,16},{128,32},{144,48},{160,128},{176,1... | collective-permute-start | bytes 1032200 | tf_op jit(solution)/shard_map/ppermute | solution.py:20
  126.1 29.9 %collective-permute-start.9 = (bf16[1,96,1792]{2,1,0:T(8,128)(2,1)S(1)}, bf16[1,96,1792]{2,1,0:T(8,128)(2,1)S(1)}, u32[]{:S(2)}, u32[]{:S(2)}) collective-permute-start(bf16[1,96,1792]{2,1,0:T(8,128)(2,1)S(1)} %get-tuple-element.16), channel_id=1, source_target_pairs={{0,32},{16,48},{32,128},{48,144},{128,160},{144,176},{160,0},{176,... | collective-permute-start | bytes 1032200 | tf_op jit(solution)/shard_map/ppermute | solution.py:20
  166.1 3.9 %copy-start.3 = (f32[64,8]{0,1:T(8,128)S(1)}, f32[64,8]{0,1:T(8,128)}, u32[]{:S(2)}) copy-start(f32[64,8]{0,1:T(8,128)} %param.8) | copy-start | bytes 6148
  166.1 44.6 %all-to-all-start.1 = ((bf16[16,48,1792]{2,1,0:T(8,128)(2,1)}), bf16[16,48,1792]{2,1,0:T(8,128)(2,1)S(1)}, u32[]{:S(2)}, u32[]{:S(2)}) async-start(bf16[16,48,1792]{2,1,0:T(8,128)(2,1)} %copy.94), calls=%async_computation.1 | async-start | bytes 5505024 | tf_op jit(solution)/shard_map/all_to_all | solution.py:117
  170.0 58.3 %copy-start.1 = (s32[64,2]{0,1:T(2,128)S(1)}, s32[64,2]{0,1:T(2,128)}, u32[]{:S(2)}) copy-start(s32[64,2]{0,1:T(2,128)} %param.9) | copy-start | bytes 1540
  212.2 15.4 %collective-permute-start.11 = (f32[64,896]{1,0:T(8,128)S(1)}, f32[64,896]{1,0:T(8,128)S(1)}, u32[]{:S(2)}, u32[]{:S(2)}) collective-permute-start(f32[64,896]{1,0:T(8,128)S(1)} %slice_select_fusion), channel_id=1, source_target_pairs={{0,128},{128,0},{1,129},{129,1},{2,130},{130,2},{3,131},{131,3},{4... | collective-permute-start | bytes 688136 | tf_op jit(solution)/shard_map/ppermute | solution.py:15
